TPU v7x, 32 devices: a whole 2x2x4 slice. The times are simulated.
32 devices in a mesh: dp: 8 (over z, y), region: 4 (over x, core).
Axes of the slice: x: 2, y: 2, z: 4, core: 2. Of those that a mesh axis runs over, the one named last changes fastest.
Arguments:
- travel_times: float32 [512, 128], P('dp'), may hold values from -60 to 60
- sensitivity: bfloat16 [512, 8, 128, 128], P('dp', 'region'), may hold values from -0.1875 to 0.1875
- tile_blocks: int32 [512, 8], P('dp', 'region'), may hold values from 0 to 1023
- face_blocks: int32 [1024, 2], P(('dp', 'region')), may hold values from 0 to 1023, as said below
- face_weights: float32 [1024, 128], P(('dp', 'region')), may hold values from 0.2 to 2
- face_count: int32 [32], P(('dp', 'region')), may hold values from 8 to 32, as said below
Outputs:
- solution: float32 [1024, 128], P('region')
Inputs may be any that keep to these rules, and one draw needn't show every extreme that they name: `face_blocks`: the first block of a face lies in the region of the device that holds the face, the second in that region or in the region one step up or down, the regions closing into a loop. `face_count`: entry k counts the faces in use among the 32 rows held by device k of dp+region; they are its first rows; some device holds 32.
All inputs are finite; a program needn't handle non-finite values.
Results may differ from a plain program's by a relative error of at most 0.0025.
The roundings to bfloat16 on the way count: a program that leaves them out, or rounds other values in their place, can miss the bound.
Values may be sent and summed in bfloat16 or wider, within the bound.
No kernel may reach another device: no remote copies, remote signals or barrier semaphores. Data moves between devices by JAX's collectives and lax.ppermute only.
A program may use at most 64 MiB of HBM per device.

v0:
```python
import jax
import jax.numpy as jnp
from jax import lax
from jax.sharding import PartitionSpec as P

ITERS = 2
NB_DEV = 256
smooth_weight = 1.0


def reduce_partials(partials):
    summed = lax.psum(partials, ("dp", "region"))
    return lax.dynamic_slice_in_dim(summed, lax.axis_index("region") * NB_DEV, NB_DEV, 0)


def piece_squares(piece):
    local_sq = jnp.sum(piece * piece)
    return lax.psum(local_sq, "region")


def model_field(piece):
    slab_half = piece.astype(jnp.bfloat16)
    return lax.all_gather(slab_half, "region", axis=0, tiled=True)


def left_squares(ray_sq, face_sq):
    return lax.psum(ray_sq, "dp") + lax.psum(face_sq, ("dp", "region"))


def local(travel_times, sensitivity, tile_blocks, face_blocks, face_weights, face_count):
    model_rows = NB_DEV * lax.axis_size("region")
    live_mask = (jnp.arange(face_blocks.shape[0]) < face_count[0]).astype(jnp.float32)
    face_scale = smooth_weight * face_weights * live_mask[:, None]
    first_block = face_blocks[:, 0]
    second_block = face_blocks[:, 1]
    flat_blocks = tile_blocks.reshape(-1)

    def transposed(left_rays, left_faces):
        rays_half = left_rays.astype(jnp.bfloat16)
        contrib = jnp.einsum(
            "tsrb,tr->tsb", sensitivity, rays_half, preferred_element_type=jnp.float32
        )
        contrib_rows = contrib.reshape(-1, contrib.shape[-1])
        face_term = face_scale * left_faces
        partials = jax.ops.segment_sum(contrib_rows, flat_blocks, num_segments=model_rows)
        partials = partials + jax.ops.segment_sum(face_term, first_block, num_segments=model_rows)
        partials = partials - jax.ops.segment_sum(face_term, second_block, num_segments=model_rows)
        return reduce_partials(partials)

    beta_value = jnp.sqrt(
        left_squares(jnp.sum(travel_times * travel_times), jnp.zeros((), jnp.float32))
    )
    left_rays = travel_times / beta_value
    left_faces = jnp.zeros(face_weights.shape, jnp.float32)
    right_vector = transposed(left_rays, left_faces)
    alpha_value = jnp.sqrt(piece_squares(right_vector))
    right_vector = right_vector / alpha_value
    direction = right_vector
    solution = jnp.zeros_like(right_vector)
    phi_bar = beta_value
    rho_bar = alpha_value
    for iteration in range(ITERS):
        full_model = model_field(right_vector)
        picked = full_model[tile_blocks]
        partial_value = jnp.einsum(
            "tsrb,tsb->tr", sensitivity, picked, preferred_element_type=jnp.float32
        )
        ray_pred = lax.psum(partial_value.astype(jnp.bfloat16), "region").astype(jnp.float32)
        face_pred = face_scale * (
            full_model[first_block].astype(jnp.float32)
            - full_model[second_block].astype(jnp.float32)
        )
        ray_pred, face_pred = (ray_pred, face_pred)
        left_rays = ray_pred - alpha_value * left_rays
        left_faces = face_pred - alpha_value * left_faces
        beta_value = jnp.sqrt(
            left_squares(jnp.sum(left_rays * left_rays), jnp.sum(left_faces * left_faces))
        )
        left_rays = left_rays / beta_value
        left_faces = left_faces / beta_value
        last_turn = iteration + 1 == ITERS
        if not last_turn:
            right_vector = transposed(left_rays, left_faces) - beta_value * right_vector
            alpha_new = jnp.sqrt(piece_squares(right_vector))
            right_vector = right_vector / alpha_new
        rho_value = jnp.sqrt(rho_bar * rho_bar + beta_value * beta_value)
        cosine = rho_bar / rho_value
        sine_value = beta_value / rho_value
        phi_value = cosine * phi_bar
        phi_bar = sine_value * phi_bar
        solution = solution + phi_value / rho_value * direction
        if not last_turn:
            rho_bar = -cosine * alpha_new
            direction = right_vector - sine_value * alpha_new / rho_value * direction
            alpha_value = alpha_new
    return solution


def solution(mesh):
    in_specs = (
        P("dp", None),
        P("dp", "region", None, None),
        P("dp", "region"),
        P(("dp", "region"), None),
        P(("dp", "region"), None),
        P(("dp", "region")),
    )
    out_specs = P("region", None)
    return jax.shard_map(local, mesh=mesh, in_specs=in_specs, out_specs=out_specs, check_vma=False)
```

profile of v0, /device:TPU:12, one launch (start us, length us, event | category | flops | bytes accessed | tf_op | source)
XLA Modules:
  0.0 539.1 jit_solution(2553015749312402894)
XLA Ops:
  6.5 0.0 copy-start.3
  6.5 0.0 all-reduce.3.cloned.1.call-start
  6.5 0.8 fusion.24
  7.3 0.8 copy.9
  8.7 1.4 multiply_reduce_fusion.4
  10.1 0.1 broadcast_in_dim_reshape.4
  10.2 15.8 %psum.84 = f32[]{:T(128)} all-reduce(f32[]{:T(128)} %multiply_reduce_fusion.4), channel_id=1, replica_groups=mesh['dp'=8,'region'=4] {'dp'}, use_global_device_ids=true, to_apply=%region_1.0 | all-reduce | flops 1 | bytes 8 | tf_op jit(solution)/shard_map/psum | solution.py:27
  26.0 46.4 %psum.85 = f32[]{:T(128)} all-reduce(f32[]{:T(128)} %constant.5.clone.1), channel_id=1, replica_groups=mesh['dp'=8,'region'=4] {'dp','region'}, use_global_device_ids=true, to_apply=%region_2.0 | all-reduce | flops 1 | bytes 8 | tf_op jit(solution)/shard_map/psum | solution.py:27
  73.8 0.8 convert_bitcast_fusion.1
  74.6 0.8 multiply_multiply_fusion.1
  75.4 1.1 scatter_custom_fusion.1
  76.5 2.8 fusion.21
  79.3 0.0 copy-start.1
  79.3 0.0 copy-start.2
  79.3 1.3 scatter_custom_fusion
  80.6 0.9 sub.30
  81.5 0.0 all-reduce.3.cloned.1.call-update
  81.5 0.0 all-reduce.5.cloned.1.call-start
  81.5 0.0 copy-done.3
  81.6 0.1 copy.10
  81.7 0.1 reshape.15
  81.8 126.7 %all-reduce.3.cloned.1.call-done = f32[1024,128]{1,0:T(8,128)} async-done(((f32[1024,128]{1,0:T(8,128)}), f32[1024,128]{1,0:T(8,128)}) %all-reduce.3.cloned.1.call-update) | async-done | bytes 524304 | tf_op jit(solution)/shard_map/psum | solution.py:12
  208.6 1.5 multiply_reduce_fusion.1
  210.1 6.3 %psum.87 = f32[]{:T(128)} all-reduce(f32[]{:T(128)} %multiply_reduce_fusion.1), channel_id=1, replica_groups=mesh['dp'=8,'region'=4] {'region'}, use_global_device_ids=true, to_apply=%region_7.0 | all-reduce | flops 1 | bytes 8 | tf_op jit(solution)/shard_map/psum | solution.py:18
  217.1 0.9 fusion.26
  218.0 5.8 %all_gather.6 = bf16[1024,128]{1,0:T(8,128)(2,1)S(1)} all-gather(bf16[256,128]{1,0:T(8,128)(2,1)S(1)} %fusion.26), channel_id=1, replica_groups=mesh['dp'=8,'region'=4] {'region'}, dimensions={0}, use_global_device_ids=true | all-gather | bytes 327680 | tf_op jit(solution)/shard_map/all_gather | solution.py:23
  223.8 0.7 gather_fusion
  224.5 3.4 fusion.16
  227.9 0.0 copy-start
  227.9 10.7 %psum.88 = bf16[64,128]{1,0:T(8,128)(2,1)S(1)} all-reduce(bf16[64,128]{1,0:T(8,128)(2,1)S(1)} %convert_element_type.46), channel_id=1, replica_groups=mesh['dp'=8,'region'=4] {'region'}, use_global_device_ids=true, to_apply=%region_8.0 | all-reduce | flops 8192 | bytes 32768 | tf_op jit(solution)/shard_map/psum | solution.py:68
  238.6 0.0 copy-done.1
  238.6 0.6 multiply_reduce_fusion.3
  239.2 0.6 gather_fusion.2
  239.8 0.6 gather_fusion.1
  240.4 0.0 copy-done.2
  240.4 0.8 multiply_reduce_fusion.6
  241.2 16.7 %psum.89 = f32[]{:T(128)} all-reduce(f32[]{:T(128)} %multiply_reduce_fusion.3), channel_id=1, replica_groups=mesh['dp'=8,'region'=4] {'dp'}, use_global_device_ids=true, to_apply=%region_10.0 | all-reduce | flops 1 | bytes 8 | tf_op jit(solution)/shard_map/psum | solution.py:27
  257.9 43.8 %psum.90 = f32[]{:T(128)} all-reduce(f32[]{:T(128)} %multiply_reduce_fusion.6), channel_id=1, replica_groups=mesh['dp'=8,'region'=4] {'dp','region'}, use_global_device_ids=true, to_apply=%region_12.0 | all-reduce | flops 1 | bytes 8 | tf_op jit(solution)/shard_map/psum | solution.py:27
  303.1 0.1 multiply_multiply_fusion
  303.2 2.8 fusion.19
  306.0 0.8 scatter_custom_fusion.3
  306.9 1.3 scatter_custom_fusion.2
  308.2 0.9 sub.34
  309.0 0.0 all-reduce.5.cloned.1.call-update
  309.2 126.8 %all-reduce.5.cloned.1.call-done = f32[1024,128]{1,0:T(8,128)} async-done(((f32[1024,128]{1,0:T(8,128)}), f32[1024,128]{1,0:T(8,128)}) %all-reduce.5.cloned.1.call-update) | async-done | bytes 524304 | tf_op jit(solution)/shard_map/psum | solution.py:12
  436.0 0.0 copy-done
  436.0 1.6 multiply_reduce_fusion
  437.6 6.3 %psum.92 = f32[]{:T(128)} all-reduce(f32[]{:T(128)} %multiply_reduce_fusion), channel_id=1, replica_groups=mesh['dp'=8,'region'=4] {'region'}, use_global_device_ids=true, to_apply=%region_17.0 | all-reduce | flops 1 | bytes 8 | tf_op jit(solution)/shard_map/psum | solution.py:18
  444.6 0.9 fusion.18
  445.6 5.8 %all_gather.7 = bf16[1024,128]{1,0:T(8,128)(2,1)S(1)} all-gather(bf16[256,128]{1,0:T(8,128)(2,1)S(1)} %fusion.18), channel_id=1, replica_groups=mesh['dp'=8,'region'=4] {'region'}, dimensions={0}, use_global_device_ids=true | all-gather | bytes 327680 | tf_op jit(solution)/shard_map/all_gather | solution.py:23
  451.3 0.7 gather_fusion.3
  452.1 0.6 gather_fusion.5
  452.6 0.6 gather_fusion.4
  453.3 3.4 fusion.14
  456.7 10.6 %psum.93 = bf16[64,128]{1,0:T(8,128)(2,1)S(1)} all-reduce(bf16[64,128]{1,0:T(8,128)(2,1)S(1)} %convert_element_type.52), channel_id=1, replica_groups=mesh['dp'=8,'region'=4] {'region'}, use_global_device_ids=true, to_apply=%region_18.0 | all-reduce | flops 8192 | bytes 32768 | tf_op jit(solution)/shard_map/psum | solution.py:68
  467.3 0.6 multiply_reduce_fusion.2
  467.9 16.7 %psum.94 = f32[]{:T(128)} all-reduce(f32[]{:T(128)} %multiply_reduce_fusion.2), channel_id=1, replica_groups=mesh['dp'=8,'region'=4] {'dp'}, use_global_device_ids=true, to_apply=%region_20.0 | all-reduce | flops 1 | bytes 8 | tf_op jit(solution)/shard_map/psum | solution.py:27
  484.6 0.8 multiply_reduce_fusion.5
  485.4 43.8 %psum.95 = f32[]{:T(128)} all-reduce(f32[]{:T(128)} %multiply_reduce_fusion.5), channel_id=1, replica_groups=mesh['dp'=8,'region'=4] {'dp','region'}, use_global_device_ids=true, to_apply=%region_22.0 | all-reduce | flops 1 | bytes 8 | tf_op jit(solution)/shard_map/psum | solution.py:27
  530.7 1.6 multiply_add_fusion
  (8 shorter events, 0.0 us)
Async XLA Ops:
  6.5 75.0 %copy-start.3 = (s32[64,2]{0,1:T(2,128)S(1)}, s32[64,2]{0,1:T(2,128)}, u32[]{:S(2)}) copy-start(s32[64,2]{0,1:T(2,128)} %param.8) | copy-start | bytes 1540
  6.5 202.0 %all-reduce.3.cloned.1.call-start = ((), (), s32[]{:S(2)}) async-start(), calls=%async_computation | async-start | bytes 1048576 | tf_op jit(solution)/shard_map/psum | solution.py:12
  79.3 159.3 %copy-start.1 = (f32[64,128]{1,0:T(8,128)S(1)}, f32[64,128]{1,0:T(8,128)}, u32[]{:S(2)}) copy-start(f32[64,128]{1,0:T(8,128)} %param.6) | copy-start | bytes 98308
  79.3 161.1 %copy-start.2 = (f32[32,128]{1,0:T(8,128)S(1)}, f32[32,128]{1,0:T(8,128)}, u32[]{:S(2)}) copy-start(f32[32,128]{1,0:T(8,128)} %param.10) | copy-start | bytes 49156
  81.5 354.5 %all-reduce.5.cloned.1.call-start = ((), (), s32[]{:S(2)}) async-start(), calls=%async_computation.1 | async-start | bytes 1048576 | tf_op jit(solution)/shard_map/psum | solution.py:12
  227.9 208.1 %copy-start = (f32[1024,128]{1,0:T(8,128)S(1)}, f32[1024,128]{1,0:T(8,128)}, u32[]{:S(2)}) copy-start(f32[1024,128]{1,0:T(8,128)} %all-reduce.3.cloned.1.call-done) | copy-start | bytes 1572868
Sparse Core Ops, SparseCore 0:
  81.6 126.9 all-reduce.2
  309.2 126.7 all-reduce.4
where the time goes:
time: 540 us; the launch traced here: 539 us
  waiting for transfers between devices  254 us (47%)
  blocking collectives  229 us (42%)
  between operations  20.1 us (4%)
  other arithmetic  19.3 us (4%)
  matrix products  12.4 us (2%)
    psum x2, waiting for transfers between devices, reduce_partials(): summed = lax.psum(partials, ('dp', 'region'))  254 us
    psum x6, blocking collectives, left_squares(): return lax.psum(ray_sq, 'dp') + lax.psum(face_sq, ('dp', 'region'))  183 us
    psum x2, blocking collectives, local(): lax.psum(partial_value.astype(jnp.bfloat16), 'region').astype(jnp.float32)  21.3 us
    psum x2, blocking collectives, piece_squares(): return lax.psum(local_sq, 'region')  12.6 us
    all_gather x2, blocking collectives, model_field(): return lax.all_gather(slab_half, 'region', axis=0, tiled=True)  11.6 us
  transfers between devices with their start and end apart: 2, of which 2 were waited for; matrix products, arithmetic and copies ran while one was open for 0% of the time, Pallas kernels for 0%

commit v1 on v0

--- a/solution.py
+++ b/solution.py
@@ -1,3 +1,4 @@
+import functools
 import jax
 import jax.numpy as jnp
 from jax import lax
@@ -6,6 +7,31 @@
 ITERS = 2
 NB_DEV = 256
 smooth_weight = 1.0
+
+
+def counts_define(my_data, link_axis):
+    w1, wide_out, parts_out = (
+        lax.psum(1, axis_name=link_axis),
+        lax.axis_index(link_axis),
+        my_data.shape[0],
+    )
+    after, x_now = (my_data, 1)
+    while x_now < w1:
+        after = jnp.concatenate(
+            [
+                after,
+                lax.ppermute(
+                    after, axis_name=link_axis, perm=[(rr, (rr - x_now) % w1) for rr in range(w1)]
+                ),
+            ],
+            0,
+        )
+        x_now = 2 * x_now
+    v_now = jnp.roll(after, wide_out * parts_out, 0)
+    return v_now
+
+
+shape_trails_in = functools.partial(counts_define, link_axis="region")
 
 
 def reduce_partials(partials):
@@ -20,7 +46,7 @@
 
 def model_field(piece):
     slab_half = piece.astype(jnp.bfloat16)
-    return lax.all_gather(slab_half, "region", axis=0, tiled=True)
+    return shape_trails_in(slab_half)
 
 
 def left_squares(ray_sq, face_sq):

time: 540 us -> 550 us (1.019)
  waiting for transfers between devices: 254 us -> 265 us
  blocking collectives: 229 us -> 219 us
    ppermute x0 -> x4, waiting for transfers between devices: none -> 12.3 us  [counts_define(): lax.ppermute(after, axis_name=link_axis, perm=[(rr, (rr - x_now) % w1) fo...]
    all_gather x2 -> x0, blocking collectives: 11.6 us -> none  [model_field(): return lax.all_gather(slab_half, 'region', axis=0, tiled=True)]
  transfers between devices with their start and end apart: 2 -> 6, of which waited for: 2 -> 6; matrix products, arithmetic and copies ran while one was open for 0% -> 0% of each run, Pallas kernels for 0% -> 0%
where the time goes in v1:
time: 550 us; the launch traced here: 549 us
  waiting for transfers between devices  265 us (48%)
  blocking collectives  219 us (40%)
  other arithmetic  24 us (4%)
  between operations  20.1 us (4%)
  matrix products  12.4 us (2%)
    psum x2, waiting for transfers between devices, reduce_partials(): summed = lax.psum(partials, ('dp', 'region'))  253 us
    psum x6, blocking collectives, left_squares(): return lax.psum(ray_sq, 'dp') + lax.psum(face_sq, ('dp', 'region'))  183 us
    psum x2, blocking collectives, local(): lax.psum(partial_value.astype(jnp.bfloat16), 'region').astype(jnp.float32)  23 us
    psum x2, blocking collectives, piece_squares(): return lax.psum(local_sq, 'region')  12.5 us
    ppermute x4, waiting for transfers between devices, counts_define(): lax.ppermute(after, axis_name=link_axis, perm=[(rr, (rr - x_now) % w1) fo...  12.3 us
  transfers between devices with their start and end apart: 6, of which 6 were waited for; matrix products, arithmetic and copies ran while one was open for 0% of the time, Pallas kernels for 0%

profile of v1, /device:TPU:12, one launch (start us, length us, event | category | flops | bytes accessed | tf_op | source)
XLA Modules:
  0.0 549.1 jit_solution(6149810120157195198)
XLA Ops:
  6.5 0.0 all-reduce.3.cloned.1.call-start
  6.5 0.8 fusion.34
  7.3 0.8 copy.9
  8.7 1.4 multiply_reduce_fusion.4
  10.1 0.1 broadcast_in_dim_reshape.4
  10.2 15.8 %psum.84 = f32[]{:T(128)} all-reduce(f32[]{:T(128)} %multiply_reduce_fusion.4), channel_id=1, replica_groups=mesh['dp'=8,'region'=4] {'dp'}, use_global_device_ids=true, to_apply=%region_1.0 | all-reduce | flops 1 | bytes 8 | tf_op jit(solution)/shard_map/psum | solution.py:53
  26.0 46.4 %psum.85 = f32[]{:T(128)} all-reduce(f32[]{:T(128)} %constant.13.clone.1), channel_id=1, replica_groups=mesh['dp'=8,'region'=4] {'dp','region'}, use_global_device_ids=true, to_apply=%region_2.0 | all-reduce | flops 1 | bytes 8 | tf_op jit(solution)/shard_map/psum | solution.py:53
  73.8 0.8 convert_bitcast_fusion.1
  74.6 0.8 multiply_multiply_fusion.1
  75.4 1.1 scatter_custom_fusion.1
  76.5 2.8 fusion.31
  79.3 1.3 scatter_custom_fusion
  80.6 0.0 copy-start.2
  80.6 0.9 sub.33
  81.4 0.0 all-reduce.3.cloned.1.call-update
  81.5 0.0 all-reduce.5.cloned.1.call-start
  81.5 127.0 %all-reduce.3.cloned.1.call-done = f32[1024,128]{1,0:T(8,128)} async-done(((f32[1024,128]{1,0:T(8,128)}), f32[1024,128]{1,0:T(8,128)}) %all-reduce.3.cloned.1.call-update) | async-done | bytes 524304 | tf_op jit(solution)/shard_map/psum | solution.py:38
  208.5 1.5 multiply_reduce_fusion.1
  210.1 6.3 %psum.87 = f32[]{:T(128)} all-reduce(f32[]{:T(128)} %multiply_reduce_fusion.1), channel_id=1, replica_groups=mesh['dp'=8,'region'=4] {'region'}, use_global_device_ids=true, to_apply=%region_7.0 | all-reduce | flops 1 | bytes 8 | tf_op jit(solution)/shard_map/psum | solution.py:44
  217.0 0.9 fusion.36
  218.0 0.2 collective-permute-start
  218.1 0.0 copy-done.3
  218.1 0.1 copy.10
  218.2 0.1 reshape.15
  218.4 1.7 collective-permute-done
  220.1 1.4 collective-permute-start.1
  221.5 4.5 collective-permute-done.1
  226.0 2.3 fusion.7
  228.4 0.7 gather_fusion
  229.1 3.4 fusion.26
  232.4 11.5 %psum.88 = bf16[64,128]{1,0:T(8,128)(2,1)S(1)} all-reduce(bf16[64,128]{1,0:T(8,128)(2,1)S(1)} %convert_element_type.46), channel_id=1, replica_groups=mesh['dp'=8,'region'=4] {'region'}, use_global_device_ids=true, to_apply=%region_8.10 | all-reduce | flops 8192 | bytes 32768 | tf_op jit(solution)/shard_map/psum | solution.py:94
  244.0 0.0 copy-done.1
  244.0 0.6 multiply_reduce_fusion.3
  244.6 0.6 gather_fusion.2
  245.2 0.6 gather_fusion.1
  245.8 0.0 copy-done.2
  245.8 0.8 multiply_reduce_fusion.6
  246.6 15.8 %psum.89 = f32[]{:T(128)} all-reduce(f32[]{:T(128)} %multiply_reduce_fusion.3), channel_id=1, replica_groups=mesh['dp'=8,'region'=4] {'dp'}, use_global_device_ids=true, to_apply=%region_10.12 | all-reduce | flops 1 | bytes 8 | tf_op jit(solution)/shard_map/psum | solution.py:53
  262.3 44.8 %psum.90 = f32[]{:T(128)} all-reduce(f32[]{:T(128)} %multiply_reduce_fusion.6), channel_id=1, replica_groups=mesh['dp'=8,'region'=4] {'dp','region'}, use_global_device_ids=true, to_apply=%region_12.14 | all-reduce | flops 1 | bytes 8 | tf_op jit(solution)/shard_map/psum | solution.py:53
  308.5 0.1 multiply_multiply_fusion
  308.6 2.8 fusion.29
  311.4 0.8 scatter_custom_fusion.3
  312.3 1.3 scatter_custom_fusion.2
  313.5 0.9 sub.37
  314.4 0.0 all-reduce.5.cloned.1.call-update
  314.4 126.1 %all-reduce.5.cloned.1.call-done = f32[1024,128]{1,0:T(8,128)} async-done(((f32[1024,128]{1,0:T(8,128)}), f32[1024,128]{1,0:T(8,128)}) %all-reduce.5.cloned.1.call-update) | async-done | bytes 524304 | tf_op jit(solution)/shard_map/psum | solution.py:38
  440.5 1.6 multiply_reduce_fusion
  442.1 6.3 %psum.92 = f32[]{:T(128)} all-reduce(f32[]{:T(128)} %multiply_reduce_fusion), channel_id=1, replica_groups=mesh['dp'=8,'region'=4] {'region'}, use_global_device_ids=true, to_apply=%region_17.19 | all-reduce | flops 1 | bytes 8 | tf_op jit(solution)/shard_map/psum | solution.py:44
  449.1 0.9 fusion.28
  450.0 0.3 collective-permute-start.2
  450.4 1.9 collective-permute-done.2
  452.3 1.4 collective-permute-start.3
  453.9 4.3 collective-permute-done.3
  458.2 2.3 fusion.2
  460.6 0.7 gather_fusion.3
  461.3 0.6 gather_fusion.5
  461.9 0.6 gather_fusion.4
  462.5 3.4 fusion.24
  465.8 11.4 %psum.93 = bf16[64,128]{1,0:T(8,128)(2,1)S(1)} all-reduce(bf16[64,128]{1,0:T(8,128)(2,1)S(1)} %convert_element_type.52), channel_id=1, replica_groups=mesh['dp'=8,'region'=4] {'region'}, use_global_device_ids=true, to_apply=%region_18.20 | all-reduce | flops 8192 | bytes 32768 | tf_op jit(solution)/shard_map/psum | solution.py:94
  477.2 0.6 multiply_reduce_fusion.2
  477.9 0.8 multiply_reduce_fusion.5
  478.6 15.8 %psum.94 = f32[]{:T(128)} all-reduce(f32[]{:T(128)} %multiply_reduce_fusion.2), channel_id=1, replica_groups=mesh['dp'=8,'region'=4] {'dp'}, use_global_device_ids=true, to_apply=%region_20.22 | all-reduce | flops 1 | bytes 8 | tf_op jit(solution)/shard_map/psum | solution.py:53
  494.4 44.8 %psum.95 = f32[]{:T(128)} all-reduce(f32[]{:T(128)} %multiply_reduce_fusion.5), channel_id=1, replica_groups=mesh['dp'=8,'region'=4] {'dp','region'}, use_global_device_ids=true, to_apply=%region_22.24 | all-reduce | flops 1 | bytes 8 | tf_op jit(solution)/shard_map/psum | solution.py:53
  540.7 1.6 multiply_add_fusion
  (14 shorter events, 0.1 us)
Async XLA Ops:
  6.5 211.6 %copy-start.3 = (s32[64,2]{0,1:T(2,128)S(1)}, s32[64,2]{0,1:T(2,128)}, u32[]{:S(2)}) copy-start(s32[64,2]{0,1:T(2,128)} %param.10) | copy-start | bytes 1540
  6.5 202.0 %all-reduce.3.cloned.1.call-start = ((), (), s32[]{:S(2)}) async-start(), calls=%async_computation | async-start | bytes 1048576 | tf_op jit(solution)/shard_map/psum | solution.py:38
  79.3 164.7 %copy-start.1 = (f32[64,128]{1,0:T(8,128)S(1)}, f32[64,128]{1,0:T(8,128)}, u32[]{:S(2)}) copy-start(f32[64,128]{1,0:T(8,128)} %param.8) | copy-start | bytes 98308
  80.6 165.2 %copy-start.2 = (f32[32,128]{1,0:T(8,128)S(1)}, f32[32,128]{1,0:T(8,128)}, u32[]{:S(2)}) copy-start(f32[32,128]{1,0:T(8,128)} %param.12) | copy-start | bytes 49156
  81.5 359.1 %all-reduce.5.cloned.1.call-start = ((), (), s32[]{:S(2)}) async-start(), calls=%async_computation.1 | async-start | bytes 1048576 | tf_op jit(solution)/shard_map/psum | solution.py:38
  218.0 2.1 collective-permute-start
  220.1 5.9 %collective-permute-start.1 = (bf16[512,128]{1,0:T(8,128)(2,1)S(1)}, bf16[512,128]{1,0:T(8,128)(2,1)S(1)}, u32[]{:S(2)}, u32[]{:S(2)}) collective-permute-start(bf16[512,128]{1,0:T(8,128)(2,1)S(1)} %pad_maximum_fusion), channel_id=1, source_target_pairs={{0,2},{1,3},{2,0},{3,1},{4,6},{5,7},{6,4},{7,5},{8,10},{9,11},{10,... | collective-permute-start | bytes 393224 | tf_op jit(solution)/shard_map/ppermute | solution.py:23
  232.4 208.1 %copy-start = (f32[1024,128]{1,0:T(8,128)S(1)}, f32[1024,128]{1,0:T(8,128)}, u32[]{:S(2)}) copy-start(f32[1024,128]{1,0:T(8,128)} %all-reduce.3.cloned.1.call-done) | copy-start | bytes 1572868
  450.0 2.3 collective-permute-start.2
  452.3 5.9 %collective-permute-start.3 = (bf16[512,128]{1,0:T(8,128)(2,1)S(1)}, bf16[512,128]{1,0:T(8,128)(2,1)S(1)}, u32[]{:S(2)}, u32[]{:S(2)}) collective-permute-start(bf16[512,128]{1,0:T(8,128)(2,1)S(1)} %pad_maximum_fusion.1), channel_id=1, source_target_pairs={{0,2},{1,3},{2,0},{3,1},{4,6},{5,7},{6,4},{7,5},{8,10},{9,11},{10,... | collective-permute-start | bytes 393224 | tf_op jit(solution)/shard_map/ppermute | solution.py:23
Sparse Core Ops, SparseCore 0:
  81.6 126.9 all-reduce.2
  314.5 125.9 all-reduce.4
